TPU v7x, 512 devices: a whole 4x8x8 slice. The times are simulated.
512 devices in a mesh: band: 16 (over y, core), dom: 32 (over z, x).
Axes of the slice: x: 4, y: 8, z: 8, core: 2. Of those that a mesh axis runs over, the one named last changes fastest.
Arguments:
- orbitals: float32 [32, 2, 256, 8, 128], P('band', None, 'dom'), may hold values from -6 to 6
- ace_vectors: float32 [16, 2, 256, 8, 128], P(None, None, 'dom'), may hold values from -0.078125 to 0.078125
- local_potential: float32 [256, 8, 128], P('dom'), may hold values from -1 to 1
- field_strength: float32 [2], replicated, may hold values from -2 to 2
- run_projectors: float32 [1024, 4, 256], P('dom'), may hold values from -0.09375 to 0.09375
- run_atom: int32 [1024], P('dom'), may hold values from 0 to 127, as said below
- run_count: int32 [1024], P('dom'), may hold values from 1 to 256, as said below
- run_start: int32 [1024], P('dom'), may hold values from 0 to 7936, as said below
- kb_energy: float32 [128], P('dom'), may hold values from 0.1 to 1
Outputs:
- propagated: float32 [32, 2, 256, 8, 128], P('band', None, 'dom')
- forces: float32 [2, 3, 128], P(None, None, 'dom')
Inputs may be any that keep to these rules, and one draw needn't show every extreme that they name: `run_atom`: atom a is owned by index a // 4 of dom. The 32 runs of one dom index name atoms of any one owner at most 2 times, and exactly 2 times for some owner. `run_count`: every dom index has a run of 256 points. `run_start`: every dom index has a run that starts at cell 8192 - 256.
All inputs are finite; a program needn't handle non-finite values.
Results may differ from a plain program's by a relative error of at most 0.0003.
Values sent between devices are 32-bit elements; how exact they have to be, the bound alone decides.
No kernel may reach another device: no remote copies, remote signals or barrier semaphores. Data moves between devices by JAX's collectives and lax.ppermute only.
A program may use at most 64 MiB of HBM per device.

v0:
```python
import jax
import jax.numpy as jnp
from jax import lax
from jax.sharding import PartitionSpec as P

STEPS = 2
TAYLOR = 4
spacing = 0.5
time_step = 0.04
highest = lax.Precision.HIGHEST


def extended_2(block, sides, width):
    for axis, dim in sides:
        count = lax.axis_size(axis)
        forward = [(i, i + 1) for i in range(count - 1)]
        backward = [(target, source) for source, target in forward]
        low = lax.ppermute(
            lax.slice_in_dim(block, block.shape[dim] - width, None, axis=dim), axis, forward
        )
        high = lax.ppermute(lax.slice_in_dim(block, 0, width, axis=dim), axis, backward)
        block = jnp.concatenate([low, block, high], axis=dim)
    return block


def laplace(extended):
    middle = extended[:, :, 2:-2]
    along_z = 16.0 * (extended[:, :, 3:-1] + extended[:, :, 1:-3]) - (
        extended[:, :, 4:] + extended[:, :, :-4]
    )
    along_x = 16.0 * (jnp.roll(middle, 1, 3) + jnp.roll(middle, -1, 3)) - (
        jnp.roll(middle, 2, 3) + jnp.roll(middle, -2, 3)
    )
    along_y = 16.0 * (jnp.roll(middle, 1, 4) + jnp.roll(middle, -1, 4)) - (
        jnp.roll(middle, 2, 4) + jnp.roll(middle, -2, 4)
    )
    return (along_z + along_x + along_y - 90.0 * middle) / (12.0 * spacing * spacing)


def projections(ace_rows, term):
    vector_count = ace_rows.shape[0]
    orbital_count = term.shape[0]
    products = lax.dot_general(
        ace_rows.reshape(vector_count * 2, -1),
        term.reshape(orbital_count * 2, -1),
        (((1,), (1,)), ((), ())),
        precision=highest,
        preferred_element_type=jnp.float32,
    )
    products = products.reshape(vector_count, 2, orbital_count, 2)
    return jnp.stack(
        [products[:, 0, :, 0] + products[:, 1, :, 1], products[:, 0, :, 1] - products[:, 1, :, 0]]
    )


def ace_weights(ace_rows, term):
    return lax.psum(projections(ace_rows, term), "dom")


def fock_term(ace_rows, weights):
    vector_count = ace_rows.shape[0]
    orbital_count = weights.shape[2]
    real_part = weights[0]
    imag_part = weights[1]
    coefficients = jnp.stack(
        [jnp.stack([real_part, imag_part], axis=-1), jnp.stack([-imag_part, real_part], axis=-1)],
        axis=1,
    )
    applied = lax.dot_general(
        coefficients.reshape(vector_count * 2, orbital_count * 2),
        ace_rows.reshape(vector_count * 2, -1),
        (((0,), (0,)), ((), ())),
        precision=highest,
        preferred_element_type=jnp.float32,
    )
    return applied.reshape((orbital_count, 2) + ace_rows.shape[2:])


def next_term(applied, degree):
    factor = time_step / degree
    return jnp.stack([factor * applied[:, 1], -factor * applied[:, 0]], axis=1)


def taylor_rounds(current, potential, ace_vectors):
    accumulated = current
    term = current
    for degree in range(1, TAYLOR + 1):
        extended = extended_2(term, (("dom", 2),), 2)
        weights = ace_weights(ace_vectors, term)
        applied = -0.5 * laplace(extended) + potential * term - fock_term(ace_vectors, weights)
        term = next_term(applied, degree)
        accumulated = accumulated + term
    return accumulated


def atom_partials(current, run_projectors, run_atom, run_count, run_start, kb_energy):
    row_count = current.shape[0] * 2
    point_count = run_projectors.shape[2]
    atom_dev = kb_energy.shape[0]
    dom_count = lax.axis_size("dom")
    slot_count = run_atom.shape[0]
    flattened = current.reshape(row_count, -1)

    def cut_run(run_begin):
        return lax.dynamic_slice_in_dim(flattened, run_begin, point_count, 1)

    pieces = jax.vmap(cut_run)(run_start)
    in_run = jnp.arange(point_count, dtype=jnp.int32)[None, :] < run_count[:, None]
    masked = jnp.where(in_run[:, None, :], run_projectors, 0.0)
    partials = jnp.einsum("scp,srp->scr", masked, pieces, precision=highest)
    capacity = 2 * slot_count // dom_count
    owner = run_atom // atom_dev
    slot_ids = jnp.arange(slot_count, dtype=jnp.int32)
    same_owner = (owner[:, None] == owner[None, :]) & (slot_ids[None, :] < slot_ids[:, None])
    owner_rank = jnp.sum(same_owner.astype(jnp.int32), axis=1)
    slot_pos = owner * capacity + owner_rank
    placement = jnp.arange(dom_count * capacity, dtype=jnp.int32)[:, None] == slot_pos[None, :]
    outgoing = jnp.einsum("ks,scr->kcr", placement.astype(jnp.float32), partials, precision=highest)
    atom_slots = jnp.max(jnp.where(placement, (run_atom % atom_dev)[None, :], -1), axis=1)
    received, received_ids = (
        lax.all_to_all(outgoing, "dom", split_axis=0, concat_axis=0, tiled=True),
        lax.all_to_all(atom_slots, "dom", split_axis=0, concat_axis=0, tiled=True),
    )
    matches = (received_ids[None, :] == jnp.arange(atom_dev, dtype=jnp.int32)[:, None]).astype(
        jnp.float32
    )
    atom_totals = jnp.einsum("ak,kcr->acr", matches, received, precision=highest)
    return (
        2.0
        * kb_energy[None, :]
        * jnp.einsum("ar,acr->ca", atom_totals[:, 0], atom_totals[:, 1:], precision=highest)
    )


def shards(
    orbitals,
    ace_vectors,
    local_potential,
    field_strength,
    run_projectors,
    run_atom,
    run_count,
    run_start,
    kb_energy,
):
    plane_count = orbitals.shape[2]
    plane_total = plane_count * lax.axis_size("dom")
    first_plane = lax.axis_index("dom") * plane_count
    height = (
        2.0
        * ((first_plane + jnp.arange(plane_count, dtype=jnp.int32)).astype(jnp.float32) + 0.5)
        / plane_total
        - 1.0
    )
    current = orbitals
    results = []
    for step_index in range(STEPS):
        strength = field_strength[step_index]
        current = taylor_rounds(
            current, local_potential + strength * height[:, None, None], ace_vectors
        )
        partial_force = atom_partials(
            current, run_projectors, run_atom, run_count, run_start, kb_energy
        )
        partial_force = lax.psum(partial_force, "band")
        results.append(partial_force)
    forces = jnp.stack(results)
    return (current, forces)


def solution(mesh):
    in_specs = (
        P("band", None, "dom", None, None),
        P(None, None, "dom", None, None),
        P("dom", None, None),
        P(),
        P("dom", None, None),
        P("dom"),
        P("dom"),
        P("dom"),
        P("dom"),
    )
    out_specs = (P("band", None, "dom", None, None), P(None, None, "dom"))
    return jax.shard_map(shards, mesh=mesh, in_specs=in_specs, out_specs=out_specs, check_vma=False)
```

profile of v0, /device:TPU:1, one launch (start us, length us, event | category | flops | bytes accessed | tf_op | source)
XLA Modules:
  0.0 938.4 jit_solution(7851821572021941752)
XLA Ops:
  2.0 4.5 collective-permute-start.1
  7.2 1.3 collective-permute-start
  10.0 14.1 %all-to-all-start = ((s32[32,2,1]{1,2,0:T(1,128)}), s32[32,2,1]{1,2,0:T(1,128)}, u32[]{:S(2)}, u32[]{:S(2)}) async-start(s32[32,2,1]{1,2,0:T(1,128)} %bitcast.89), calls=%async_computation | async-start | bytes 32768 | tf_op jit(solution)/shard_map/all_to_all | solution.py:122
  24.2 5.0 convolution_bitcast_fusion
  29.2 60.4 %psum.70 = f32[2,16,2]{1,2,0:T(2,128)S(1)} all-reduce(f32[2,16,2]{1,2,0:T(2,128)S(1)} %pad_maximum_fusion.23), channel_id=1, replica_groups=mesh['band'=16,'dom'=32] {'dom'}, use_global_device_ids=true, to_apply=%region_0.0 | all-reduce | flops 64 | bytes 512 | tf_op jit(solution)/shard_map/psum | solution.py:57
  96.3 1.2 broadcast_multiply_fusion.1
  111.2 1.4 reduce.31
  115.1 2.7 convolution_subtract_fusion.7
  119.4 55.7 %psum.71 = f32[2,16,2]{1,2,0:T(2,128)S(1)} all-reduce(f32[2,16,2]{1,2,0:T(2,128)S(1)} %pad_maximum_fusion.26), channel_id=1, replica_groups=mesh['band'=16,'dom'=32] {'dom'}, use_global_device_ids=true, to_apply=%region_1.2 | all-reduce | flops 64 | bytes 512 | tf_op jit(solution)/shard_map/psum | solution.py:57
  180.3 1.5 collective-permute-start.2
  181.8 4.6 collective-permute-start.3
  188.8 2.0 convolution_subtract_fusion.6
  192.4 57.9 %psum.72 = f32[2,16,2]{1,2,0:T(2,128)S(1)} all-reduce(f32[2,16,2]{1,2,0:T(2,128)S(1)} %pad_maximum_fusion.29), channel_id=1, replica_groups=mesh['band'=16,'dom'=32] {'dom'}, use_global_device_ids=true, to_apply=%region_2.3 | all-reduce | flops 64 | bytes 512 | tf_op jit(solution)/shard_map/psum | solution.py:57
  256.1 1.3 collective-permute-start.4
  257.4 4.6 collective-permute-start.5
  263.7 2.8 convolution_subtract_fusion.5
  268.1 57.5 %psum.73 = f32[2,16,2]{1,2,0:T(2,128)S(1)} all-reduce(f32[2,16,2]{1,2,0:T(2,128)S(1)} %pad_maximum_fusion.32), channel_id=1, replica_groups=mesh['band'=16,'dom'=32] {'dom'}, use_global_device_ids=true, to_apply=%region_3.4 | all-reduce | flops 64 | bytes 512 | tf_op jit(solution)/shard_map/psum | solution.py:57
  327.5 1.1 fusion.42
  331.5 1.3 collective-permute-start.6
  332.8 4.8 collective-permute-start.7
  339.8 2.9 convolution_subtract_fusion.4
  344.7 57.5 %psum.74 = f32[2,16,2]{1,2,0:T(2,128)S(1)} all-reduce(f32[2,16,2]{1,2,0:T(2,128)S(1)} %pad_maximum_fusion.35), channel_id=1, replica_groups=mesh['band'=16,'dom'=32] {'dom'}, use_global_device_ids=true, to_apply=%region_4.5 | all-reduce | flops 64 | bytes 512 | tf_op jit(solution)/shard_map/psum | solution.py:57
  408.9 43.4 %while.2 = (s32[]{:T(128)}, f32[4,8192]{1,0:T(4,128)S(1)}, s32[32,2]{0,1:T(2,128)S(1)}, f32[32,4,256]{2,1,0:T(4,128)S(1)}, s32[]{:T(128)}) while((s32[]{:T(128)}, f32[4,8192]{1,0:T(4,128)S(1)}, s32[32,2]{0,1:T(2,128)S(1)}, f32[32,4,256]{2,1,0:T(4,128)S(1)}, s32[]{:T(128)}) %tuple.152), condition=%wide.while_cond, body=%wide.while_body.sunk | while | flops 2 | bytes 8297 | solution.py:105
  454.4 16.1 %all-to-all-start.1 = ((f32[64,4,4]{2,1,0:T(4,128)}), f32[64,4,4]{2,1,0:T(4,128)S(1)}, u32[]{:S(2)}, u32[]{:S(2)}) async-start(f32[64,4,4]{2,1,0:T(4,128)} %copy.269), calls=%async_computation.1 | async-start | bytes 262144 | tf_op jit(solution)/shard_map/all_to_all | solution.py:121
  471.4 3.9 collective-permute-start.9
  475.3 1.3 collective-permute-start.8
  476.6 3.2 all-to-all-done.1
  481.9 3.3 convolution_subtract_fusion.3
  486.8 58.0 %psum.75 = f32[2,16,2]{1,2,0:T(2,128)S(1)} all-reduce(f32[2,16,2]{1,2,0:T(2,128)S(1)} %pad_maximum_fusion.38), channel_id=1, replica_groups=mesh['band'=16,'dom'=32] {'dom'}, use_global_device_ids=true, to_apply=%region_5.6 | all-reduce | flops 64 | bytes 512 | tf_op jit(solution)/shard_map/psum | solution.py:57
  544.8 1.1 fusion.37
  545.9 1.1 fusion.38
  551.4 1.3 collective-permute-start.10
  552.7 5.0 collective-permute-start.11
  561.1 3.1 convolution_subtract_fusion.2
  565.8 56.2 %psum.76 = f32[2,16,2]{1,2,0:T(2,128)S(1)} all-reduce(f32[2,16,2]{1,2,0:T(2,128)S(1)} %pad_maximum_fusion.41), channel_id=1, replica_groups=mesh['band'=16,'dom'=32] {'dom'}, use_global_device_ids=true, to_apply=%region_6.7 | all-reduce | flops 64 | bytes 512 | tf_op jit(solution)/shard_map/psum | solution.py:57
  623.1 1.1 fusion.30
  624.5 1.1 fusion.26
  629.3 1.3 collective-permute-start.12
  630.6 4.6 collective-permute-start.13
  638.6 3.2 convolution_subtract_fusion.1
  643.3 56.6 %psum.77 = f32[2,16,2]{1,2,0:T(2,128)S(1)} all-reduce(f32[2,16,2]{1,2,0:T(2,128)S(1)} %pad_maximum_fusion.44), channel_id=1, replica_groups=mesh['band'=16,'dom'=32] {'dom'}, use_global_device_ids=true, to_apply=%region_7.8 | all-reduce | flops 64 | bytes 512 | tf_op jit(solution)/shard_map/psum | solution.py:57
  704.5 1.3 collective-permute-start.14
  705.8 4.7 collective-permute-start.15
  712.8 2.0 convolution_subtract_fusion
  716.6 39.1 %while.3 = (s32[]{:T(128)}, f32[4,8192]{1,0:T(4,128)S(1)}, s32[32,2]{0,1:T(2,128)S(1)}, f32[32,4,256]{2,1,0:T(4,128)S(1)}, s32[]{:T(128)}) while((s32[]{:T(128)}, f32[4,8192]{1,0:T(4,128)S(1)}, s32[32,2]{0,1:T(2,128)S(1)}, f32[32,4,256]{2,1,0:T(4,128)S(1)}, s32[]{:T(128)}) %tuple.158), condition=%wide.while_cond.1, body=%wide.while_body.1.sunk | while | flops 2 | bytes 8297 | solution.py:105
  757.8 20.5 %all-to-all-start.2 = ((f32[64,4,4]{2,1,0:T(4,128)}), f32[64,4,4]{2,1,0:T(4,128)S(1)}, u32[]{:S(2)}, u32[]{:S(2)}) async-start(f32[64,4,4]{2,1,0:T(4,128)} %copy.273), calls=%async_computation.2 | async-start | bytes 262144 | tf_op jit(solution)/shard_map/all_to_all | solution.py:121
  778.6 9.1 all-to-all-done.2
  788.7 149.0 %all-reduce.1 = (f32[1,3,4]{2,1,0:T(4,128)S(1)}, f32[1,3,4]{2,1,0:T(4,128)S(1)}) all-reduce(f32[1,3,4]{2,1,0:T(4,128)S(1)} %get-tuple-element.269, f32[1,3,4]{2,1,0:T(4,128)S(1)} %get-tuple-element.268), channel_id=1, replica_groups=mesh['band'=16,'dom'=32] {'band'}, use_global_device_ids=true, to_apply=%region_11.12 | all-reduce | flops 24 | bytes 192 | tf_op jit(solution)/shard_map/psum | solution.py:165
  (621 shorter events, 181.7 us)
Async XLA Ops:
  1.4 22.7 %copy-start = (f32[2,2,8,8,128]{4,3,2,1,0:T(8,128)S(1)}, f32[2,2,8,8,128]{4,3,2,1,0:T(8,128)}, u32[]{:S(2)}) copy-start(f32[2,2,8,8,128]{4,3,2,1,0:T(8,128)} %param.9) | copy-start | bytes 393220
  2.0 111.2 %collective-permute-start.1 = (f32[2,2,2,8,128]{4,1,3,2,0:T(2,128)}, f32[2,2,2,8,128]{4,1,3,2,0:T(2,128)}, u32[]{:S(2)}, u32[]{:S(2)}) collective-permute-start(f32[2,2,2,8,128]{4,1,3,2,0:T(2,128)} %copy.378), channel_id=1, source_target_pairs={{0,1},{1,2},{2,3},{3,4},{4,5},{5,6},{6,7},{7,8},{8,9},{9,10},{10,1... | collective-permute-start | bytes 98312 | tf_op jit(solution)/shard_map/ppermute | solution.py:18
  6.6 1.9 copy-start.71
  7.2 107.0 %collective-permute-start = (f32[2,2,2,8,128]{4,1,3,2,0:T(2,128)}, f32[2,2,2,8,128]{4,1,3,2,0:T(2,128)}, u32[]{:S(2)}, u32[]{:S(2)}) collective-permute-start(f32[2,2,2,8,128]{4,1,3,2,0:T(2,128)} %copy.379), channel_id=1, source_target_pairs={{1,0},{2,1},{3,2},{4,3},{5,4},{6,5},{7,6},{8,7},{9,8},{10,9},{11,1... | collective-permute-start | bytes 98312 | tf_op jit(solution)/shard_map/ppermute | solution.py:21
  10.0 100.7 %all-to-all-start = ((s32[32,2,1]{1,2,0:T(1,128)}), s32[32,2,1]{1,2,0:T(1,128)}, u32[]{:S(2)}, u32[]{:S(2)}) async-start(s32[32,2,1]{1,2,0:T(1,128)} %bitcast.89), calls=%async_computation | async-start | bytes 32768 | tf_op jit(solution)/shard_map/all_to_all | solution.py:122
  91.7 6.5 copy-start.1
  93.8 1.3 copy-start.72
  93.8 1.9 copy-start.68
  93.8 1.9 copy-start.73
  94.5 3.0 copy-start.44
  106.3 2.1 copy-start.11
  113.3 1.8 copy-start.52
  113.3 1.8 copy-start.53
  180.3 6.3 collective-permute-start.2
  181.8 5.3 collective-permute-start.3
  186.6 1.5 copy-start.28
  186.6 1.5 copy-start.29
  186.6 1.5 copy-start.38
  186.6 1.5 copy-start.39
  256.1 6.1 collective-permute-start.4
  257.4 5.3 collective-permute-start.5
  262.2 1.5 copy-start.20
  262.2 1.5 copy-start.30
  262.2 1.5 copy-start.31
  262.2 1.5 copy-start.40
  262.3 1.5 copy-start.41
  331.5 6.3 collective-permute-start.6
  332.8 5.3 collective-permute-start.7
  337.8 1.3 copy-start.15
  337.8 1.3 copy-start.21
  337.8 1.3 copy-start.22
  408.8 43.5 %copy-start.9 = (f32[32,4,256]{2,1,0:T(4,128)S(1)}, f32[32,4,256]{2,1,0:T(4,128)}, u32[]{:S(2)}) copy-start(f32[32,4,256]{2,1,0:T(4,128)} %param.13) | copy-start | bytes 393220
  454.4 25.4 %all-to-all-start.1 = ((f32[64,4,4]{2,1,0:T(4,128)}), f32[64,4,4]{2,1,0:T(4,128)S(1)}, u32[]{:S(2)}, u32[]{:S(2)}) async-start(f32[64,4,4]{2,1,0:T(4,128)} %copy.269), calls=%async_computation.1 | async-start | bytes 262144 | tf_op jit(solution)/shard_map/all_to_all | solution.py:121
  471.4 9.8 %copy-start.27 = (f32[2,2,8,8,126]{4,1,3,2,0:T(2,128)S(1)}, f32[2,2,8,8,126]{4,1,3,2,0:T(2,128)}, u32[]{:S(2)}) copy-start(f32[2,2,8,8,126]{4,1,3,2,0:T(2,128)} %get-tuple-element.142) | copy-start | bytes 387076
  471.4 9.8 %collective-permute-start.9 = (f32[2,2,2,8,128]{4,1,3,2,0:T(2,128)}, f32[2,2,2,8,128]{4,1,3,2,0:T(2,128)}, u32[]{:S(2)}, u32[]{:S(2)}) collective-permute-start(f32[2,2,2,8,128]{4,1,3,2,0:T(2,128)} %get-tuple-element.127), channel_id=1, source_target_pairs={{0,1},{1,2},{2,3},{3,4},{4,5},{5,6},{6,7},{7,8},{8,9},{9,10},{10,1... | collective-permute-start | bytes 98312 | tf_op jit(solution)/shard_map/ppermute | solution.py:18
  475.3 5.9 collective-permute-start.8
  551.4 7.9 collective-permute-start.10
  552.7 6.6 collective-permute-start.11
  629.3 7.5 collective-permute-start.12
  630.6 6.2 collective-permute-start.13
  704.5 6.3 collective-permute-start.14
  705.8 5.3 collective-permute-start.15
  710.7 1.3 copy-start.35
  710.8 1.3 copy-start.36
  757.8 20.5 %slice-start = ((f32[4,4,4]{2,0,1:T(4,128)}), f32[4,3,4]{2,0,1:T(4,128)S(1)}, s32[]{:S(2)}) async-start(f32[4,4,4]{2,0,1:T(4,128)} %copy-done.51), calls=%async_computation.3 | async-start | bytes 12288 | tf_op jit(solution)/shard_map/slice | solution.py:131
  757.8 20.5 %copy-start.66 = (f32[4,1,4]{2,0,1:T(4,128)S(1)}, f32[4,1,4]{2,0,1:T(4,128)}, u32[]{:S(2)}) copy-start(f32[4,1,4]{2,0,1:T(4,128)} %slice.1403) | copy-start | bytes 196
  757.8 29.9 %all-to-all-start.2 = ((f32[64,4,4]{2,1,0:T(4,128)}), f32[64,4,4]{2,1,0:T(4,128)S(1)}, u32[]{:S(2)}, u32[]{:S(2)}) async-start(f32[64,4,4]{2,1,0:T(4,128)} %copy.273), calls=%async_computation.2 | async-start | bytes 262144 | tf_op jit(solution)/shard_map/all_to_all | solution.py:121
  778.5 9.2 copy-start.65
  (49 other events, 43.5 us)
where the time goes:
time: 950 us; the launch traced here: 938 us
  blocking collectives  609 us (64%)
  local copies, waits for them, and re-layouts  129 us (14%)
  starting transfers between devices  97.9 us (10%)
  other arithmetic  50.1 us (5%)
  matrix products  36 us (4%)
  waiting for transfers between devices  13.9 us (1%)
    psum x8, blocking collectives, ace_weights(): return lax.psum(projections(ace_rows, term), 'dom')  460 us
    psum x1, blocking collectives, shards(): partial_force = lax.psum(partial_force, 'band')  149 us
    gather x192, local copies, waits for them, and re-layouts  82.4 us
    ppermute x8, starting transfers between devices, extended_2(): lax.ppermute(lax.slice_in_dim(block, block.shape[dim] - width, None, axis...  36.6 us
    all_to_all x2, starting transfers between devices, atom_partials(): lax.all_to_all(outgoing, 'dom', split_axis=0, concat_axis=0, tiled=True)  36.6 us
    another operation x60, other arithmetic, next_term(): return jnp.stack([factor * applied[:, 1], -factor * applied[:, 0]], axis=1)  35.7 us
    unnamed x177, local copies, waits for them, and re-layouts  22.7 us
    dot_general x8, matrix products, fock_term(): lax.dot_general(coefficients.reshape(vector_count * 2, orbital_count * 2)...  22.2 us
  transfers between devices with their start and end apart: 19, of which 6 were waited for; matrix products, arithmetic and copies ran while one was open for 3% of the time, Pallas kernels for 0%

commit v1 on v0

--- a/solution.py
+++ b/solution.py
@@ -8,6 +8,11 @@
 spacing = 0.5
 time_step = 0.04
 highest = lax.Precision.HIGHEST
+
+
+def define_the_units(s0, chip_axis):
+    local_next = lax.all_gather(s0, chip_axis).sum(axis=0)
+    return local_next
 
 
 def extended_2(block, sides, width):
@@ -54,7 +59,7 @@
 
 
 def ace_weights(ace_rows, term):
-    return lax.psum(projections(ace_rows, term), "dom")
+    return define_the_units(projections(ace_rows, term), "dom")
 
 
 def fock_term(ace_rows, weights):

time: 950 us -> 765 us (0.81)
  blocking collectives: 609 us -> 442 us
  starting transfers between devices: 97.9 us -> 79.5 us
    psum x8 -> x0, blocking collectives: 460 us -> none  [ace_weights(): return lax.psum(projections(ace_rows, term), 'dom')]
    all_gather x0 -> x8, blocking collectives: none -> 309 us  [define_the_units(): local_next = lax.all_gather(s0, chip_axis).sum(axis=0)]
    all_to_all x2, starting transfers between devices: 36.6 us -> 18.6 us  [atom_partials(): lax.all_to_all(outgoing, 'dom', split_axis=0, concat_axis=0, tiled=True)]
    psum x1, blocking collectives: 149 us -> 133 us  [shards(): partial_force = lax.psum(partial_force, 'band')]
  transfers between devices with their start and end apart: 19 -> 19, of which waited for: 6 -> 6; matrix products, arithmetic and copies ran while one was open for 3% -> 4% of each run, Pallas kernels for 0% -> 0%
where the time goes in v1:
time: 765 us; the launch traced here: 754 us
  blocking collectives  442 us (58%)
  local copies, waits for them, and re-layouts  129 us (17%)
  starting transfers between devices  79.5 us (10%)
  other arithmetic  50.6 us (7%)
  matrix products  36 us (5%)
  waiting for transfers between devices  14.2 us (2%)
    all_gather x8, blocking collectives, define_the_units(): local_next = lax.all_gather(s0, chip_axis).sum(axis=0)  309 us
    psum x1, blocking collectives, shards(): partial_force = lax.psum(partial_force, 'band')  133 us
    gather x192, local copies, waits for them, and re-layouts  82.4 us
    ppermute x8, starting transfers between devices, extended_2(): lax.ppermute(lax.slice_in_dim(block, block.shape[dim] - width, None, axis...  36.1 us
    another operation x60, other arithmetic, next_term(): return jnp.stack([factor * applied[:, 1], -factor * applied[:, 0]], axis=1)  35.7 us
    unnamed x177, local copies, waits for them, and re-layouts  22.7 us
    dot_general x8, matrix products, fock_term(): lax.dot_general(coefficients.reshape(vector_count * 2, orbital_count * 2)...  22.2 us
    all_to_all x2, starting transfers between devices, atom_partials(): lax.all_to_all(outgoing, 'dom', split_axis=0, concat_axis=0, tiled=True)  18.6 us
  transfers between devices with their start and end apart: 19, of which 6 were waited for; matrix products, arithmetic and copies ran while one was open for 4% of the time, Pallas kernels for 0%

profile of v1, /device:TPU:1, one launch (start us, length us, event | category | flops | bytes accessed | tf_op | source)
XLA Modules:
  0.0 754.5 jit_solution(955985360155348435)
XLA Ops:
  2.0 4.5 collective-permute-start.1
  7.2 1.3 collective-permute-start
  10.0 14.1 %all-to-all-start = ((s32[32,2,1]{1,2,0:T(1,128)}), s32[32,2,1]{1,2,0:T(1,128)}, u32[]{:S(2)}, u32[]{:S(2)}) async-start(s32[32,2,1]{1,2,0:T(1,128)} %bitcast.97), calls=%async_computation | async-start | bytes 32768 | tf_op jit(solution)/shard_map/all_to_all | solution.py:127
  24.2 5.0 convolution_bitcast_fusion
  29.2 37.1 %all-gather = f32[64,16,2]{1,2,0:T(2,128)S(1)} all-gather(f32[2,16,2]{1,2,0:T(2,128)S(1)} %pad_maximum_fusion.23), channel_id=2, replica_groups=mesh['band'=16,'dom'=32] {'dom'}, dimensions={0}, use_global_device_ids=true | all-gather | bytes 8448 | tf_op jit(solution)/shard_map/all_gather | solution.py:14
  73.0 1.2 broadcast_multiply_fusion.1
  88.0 1.4 reduce.31
  91.9 2.7 convolution_subtract_fusion.7
  96.2 35.4 %all-gather.1 = f32[64,16,2]{1,2,0:T(2,128)S(1)} all-gather(f32[2,16,2]{1,2,0:T(2,128)S(1)} %pad_maximum_fusion.26), channel_id=3, replica_groups=mesh['band'=16,'dom'=32] {'dom'}, dimensions={0}, use_global_device_ids=true | all-gather | bytes 8448 | tf_op jit(solution)/shard_map/all_gather | solution.py:14
  136.8 1.3 collective-permute-start.2
  138.1 4.6 collective-permute-start.3
  145.1 2.0 convolution_subtract_fusion.6
  148.7 38.9 %all-gather.2 = f32[64,16,2]{1,2,0:T(2,128)S(1)} all-gather(f32[2,16,2]{1,2,0:T(2,128)S(1)} %pad_maximum_fusion.29), channel_id=4, replica_groups=mesh['band'=16,'dom'=32] {'dom'}, dimensions={0}, use_global_device_ids=true | all-gather | bytes 8448 | tf_op jit(solution)/shard_map/all_gather | solution.py:14
  193.5 1.3 collective-permute-start.4
  194.8 4.6 collective-permute-start.5
  201.1 2.8 convolution_subtract_fusion.5
  205.5 41.6 %all-gather.3 = f32[64,16,2]{1,2,0:T(2,128)S(1)} all-gather(f32[2,16,2]{1,2,0:T(2,128)S(1)} %pad_maximum_fusion.32), channel_id=5, replica_groups=mesh['band'=16,'dom'=32] {'dom'}, dimensions={0}, use_global_device_ids=true | all-gather | bytes 8448 | tf_op jit(solution)/shard_map/all_gather | solution.py:14
  249.0 1.1 fusion.42
  253.0 1.3 collective-permute-start.6
  254.3 4.6 collective-permute-start.7
  261.3 2.9 convolution_subtract_fusion.4
  266.2 39.6 %all-gather.4 = f32[64,16,2]{1,2,0:T(2,128)S(1)} all-gather(f32[2,16,2]{1,2,0:T(2,128)S(1)} %pad_maximum_fusion.35), channel_id=6, replica_groups=mesh['band'=16,'dom'=32] {'dom'}, dimensions={0}, use_global_device_ids=true | all-gather | bytes 8448 | tf_op jit(solution)/shard_map/all_gather | solution.py:14
  312.5 43.4 %while.2 = (s32[]{:T(128)}, f32[4,8192]{1,0:T(4,128)S(1)}, s32[32,2]{0,1:T(2,128)S(1)}, f32[32,4,256]{2,1,0:T(4,128)S(1)}, s32[]{:T(128)}) while((s32[]{:T(128)}, f32[4,8192]{1,0:T(4,128)S(1)}, s32[32,2]{0,1:T(2,128)S(1)}, f32[32,4,256]{2,1,0:T(4,128)S(1)}, s32[]{:T(128)}) %tuple.152), condition=%wide.while_cond, body=%wide.while_body.sunk | while | flops 2 | bytes 8297 | solution.py:110
  358.0 7.4 all-to-all-start.1
  366.3 3.9 collective-permute-start.9
  370.2 1.7 collective-permute-start.8
  371.9 3.0 all-to-all-done.1
  377.1 3.3 convolution_subtract_fusion.3
  382.0 36.9 %all-gather.5 = f32[64,16,2]{1,2,0:T(2,128)S(1)} all-gather(f32[2,16,2]{1,2,0:T(2,128)S(1)} %pad_maximum_fusion.38), channel_id=7, replica_groups=mesh['band'=16,'dom'=32] {'dom'}, dimensions={0}, use_global_device_ids=true | all-gather | bytes 8448 | tf_op jit(solution)/shard_map/all_gather | solution.py:14
  418.9 1.1 fusion.37
  420.0 1.1 fusion.38
  425.5 1.3 collective-permute-start.10
  426.8 4.6 collective-permute-start.11
  434.8 3.1 convolution_subtract_fusion.2
  439.5 40.4 %all-gather.6 = f32[64,16,2]{1,2,0:T(2,128)S(1)} all-gather(f32[2,16,2]{1,2,0:T(2,128)S(1)} %pad_maximum_fusion.41), channel_id=8, replica_groups=mesh['band'=16,'dom'=32] {'dom'}, dimensions={0}, use_global_device_ids=true | all-gather | bytes 8448 | tf_op jit(solution)/shard_map/all_gather | solution.py:14
  481.0 1.1 fusion.30
  482.5 1.1 fusion.26
  487.2 1.3 collective-permute-start.12
  488.5 4.7 collective-permute-start.13
  496.7 3.2 convolution_subtract_fusion.1
  501.4 39.3 %all-gather.7 = f32[64,16,2]{1,2,0:T(2,128)S(1)} all-gather(f32[2,16,2]{1,2,0:T(2,128)S(1)} %pad_maximum_fusion.44), channel_id=9, replica_groups=mesh['band'=16,'dom'=32] {'dom'}, dimensions={0}, use_global_device_ids=true | all-gather | bytes 8448 | tf_op jit(solution)/shard_map/all_gather | solution.py:14
  545.3 1.3 collective-permute-start.14
  546.6 4.6 collective-permute-start.15
  553.6 2.0 convolution_subtract_fusion
  557.4 39.1 %while.3 = (s32[]{:T(128)}, f32[4,8192]{1,0:T(4,128)S(1)}, s32[32,2]{0,1:T(2,128)S(1)}, f32[32,4,256]{2,1,0:T(4,128)S(1)}, s32[]{:T(128)}) while((s32[]{:T(128)}, f32[4,8192]{1,0:T(4,128)S(1)}, s32[32,2]{0,1:T(2,128)S(1)}, f32[32,4,256]{2,1,0:T(4,128)S(1)}, s32[]{:T(128)}) %tuple.158), condition=%wide.while_cond.1, body=%wide.while_body.1.sunk | while | flops 2 | bytes 8297 | solution.py:110
  598.6 11.2 %all-to-all-start.2 = ((f32[64,4,4]{2,1,0:T(4,128)}), f32[64,4,4]{2,1,0:T(4,128)S(1)}, u32[]{:S(2)}, u32[]{:S(2)}) async-start(f32[64,4,4]{2,1,0:T(4,128)} %copy.273), calls=%async_computation.2 | async-start | bytes 262144 | tf_op jit(solution)/shard_map/all_to_all | solution.py:126
  610.0 9.2 %all-to-all-done.2 = f32[64,4,4]{2,1,0:T(4,128)S(1)} async-done(((f32[64,4,4]{2,1,0:T(4,128)}), f32[64,4,4]{2,1,0:T(4,128)S(1)}, u32[]{:S(2)}, u32[]{:S(2)}) %all-to-all-start.2) | async-done | bytes 4128 | tf_op jit(solution)/shard_map/all_to_all | solution.py:126
  620.2 133.5 %all-reduce.1 = (f32[1,3,4]{2,1,0:T(4,128)S(1)}, f32[1,3,4]{2,1,0:T(4,128)S(1)}) all-reduce(f32[1,3,4]{2,1,0:T(4,128)S(1)} %get-tuple-element.269, f32[1,3,4]{2,1,0:T(4,128)S(1)} %get-tuple-element.268), channel_id=1, replica_groups=mesh['band'=16,'dom'=32] {'band'}, use_global_device_ids=true, to_apply=%region_11.12 | all-reduce | flops 24 | bytes 192 | tf_op jit(solution)/shard_map/psum | solution.py:170
  (629 shorter events, 182.5 us)
Async XLA Ops:
  1.4 22.7 %copy-start = (f32[2,2,8,8,128]{4,3,2,1,0:T(8,128)S(1)}, f32[2,2,8,8,128]{4,3,2,1,0:T(8,128)}, u32[]{:S(2)}) copy-start(f32[2,2,8,8,128]{4,3,2,1,0:T(8,128)} %param.9) | copy-start | bytes 393220
  2.0 88.0 %collective-permute-start.1 = (f32[2,2,2,8,128]{4,1,3,2,0:T(2,128)}, f32[2,2,2,8,128]{4,1,3,2,0:T(2,128)}, u32[]{:S(2)}, u32[]{:S(2)}) collective-permute-start(f32[2,2,2,8,128]{4,1,3,2,0:T(2,128)} %copy.378), channel_id=1, source_target_pairs={{0,1},{1,2},{2,3},{3,4},{4,5},{5,6},{6,7},{7,8},{8,9},{9,10},{10,1... | collective-permute-start | bytes 98312 | tf_op jit(solution)/shard_map/ppermute | solution.py:23
  6.6 1.9 copy-start.71
  7.2 83.8 %collective-permute-start = (f32[2,2,2,8,128]{4,1,3,2,0:T(2,128)}, f32[2,2,2,8,128]{4,1,3,2,0:T(2,128)}, u32[]{:S(2)}, u32[]{:S(2)}) collective-permute-start(f32[2,2,2,8,128]{4,1,3,2,0:T(2,128)} %copy.379), channel_id=1, source_target_pairs={{1,0},{2,1},{3,2},{4,3},{5,4},{6,5},{7,6},{8,7},{9,8},{10,9},{11,1... | collective-permute-start | bytes 98312 | tf_op jit(solution)/shard_map/ppermute | solution.py:26
  10.0 77.4 %all-to-all-start = ((s32[32,2,1]{1,2,0:T(1,128)}), s32[32,2,1]{1,2,0:T(1,128)}, u32[]{:S(2)}, u32[]{:S(2)}) async-start(s32[32,2,1]{1,2,0:T(1,128)} %bitcast.97), calls=%async_computation | async-start | bytes 32768 | tf_op jit(solution)/shard_map/all_to_all | solution.py:127
  68.5 6.5 copy-start.1
  70.5 1.9 copy-start.68
  70.5 1.9 copy-start.73
  71.3 3.0 copy-start.44
  83.1 2.1 copy-start.11
  90.0 1.8 copy-start.52
  90.0 1.8 copy-start.53
  136.8 6.1 collective-permute-start.2
  138.1 5.3 collective-permute-start.3
  142.9 1.5 copy-start.28
  142.9 1.5 copy-start.29
  142.9 1.5 copy-start.38
  142.9 1.5 copy-start.39
  193.5 6.1 collective-permute-start.4
  194.8 5.3 collective-permute-start.5
  199.6 1.5 copy-start.20
  199.6 1.5 copy-start.30
  199.6 1.5 copy-start.31
  199.6 1.5 copy-start.40
  199.6 1.5 copy-start.41
  253.0 6.1 collective-permute-start.6
  254.3 5.3 collective-permute-start.7
  259.1 1.5 copy-start.15
  259.1 1.5 copy-start.21
  259.1 1.5 copy-start.22
  259.1 1.5 copy-start.37
  312.5 43.5 %copy-start.9 = (f32[32,4,256]{2,1,0:T(4,128)S(1)}, f32[32,4,256]{2,1,0:T(4,128)}, u32[]{:S(2)}) copy-start(f32[32,4,256]{2,1,0:T(4,128)} %param.13) | copy-start | bytes 393220
  358.0 16.9 %all-to-all-start.1 = ((f32[64,4,4]{2,1,0:T(4,128)}), f32[64,4,4]{2,1,0:T(4,128)S(1)}, u32[]{:S(2)}, u32[]{:S(2)}) async-start(f32[64,4,4]{2,1,0:T(4,128)} %copy.269), calls=%async_computation.1 | async-start | bytes 262144 | tf_op jit(solution)/shard_map/all_to_all | solution.py:126
  366.3 10.1 %copy-start.27 = (f32[2,2,8,8,126]{4,1,3,2,0:T(2,128)S(1)}, f32[2,2,8,8,126]{4,1,3,2,0:T(2,128)}, u32[]{:S(2)}) copy-start(f32[2,2,8,8,126]{4,1,3,2,0:T(2,128)} %get-tuple-element.142) | copy-start | bytes 387076
  366.3 10.0 %collective-permute-start.9 = (f32[2,2,2,8,128]{4,1,3,2,0:T(2,128)}, f32[2,2,2,8,128]{4,1,3,2,0:T(2,128)}, u32[]{:S(2)}, u32[]{:S(2)}) collective-permute-start(f32[2,2,2,8,128]{4,1,3,2,0:T(2,128)} %get-tuple-element.127), channel_id=1, source_target_pairs={{0,1},{1,2},{2,3},{3,4},{4,5},{5,6},{6,7},{7,8},{8,9},{9,10},{10,1... | collective-permute-start | bytes 98312 | tf_op jit(solution)/shard_map/ppermute | solution.py:23
  370.2 6.2 collective-permute-start.8
  425.5 7.5 collective-permute-start.10
  426.8 6.2 collective-permute-start.11
  487.2 7.7 %collective-permute-start.12 = (f32[2,2,2,8,128]{4,1,3,2,0:T(2,128)}, f32[2,2,2,8,128]{4,1,3,2,0:T(2,128)}, u32[]{:S(2)}, u32[]{:S(2)}) collective-permute-start(f32[2,2,2,8,128]{4,1,3,2,0:T(2,128)} %get-tuple-element.84), channel_id=1, source_target_pairs={{1,0},{2,1},{3,2},{4,3},{5,4},{6,5},{7,6},{8,7},{9,8},{10,9},{11,1... | collective-permute-start | bytes 98312 | tf_op jit(solution)/shard_map/ppermute | solution.py:26
  488.5 6.4 collective-permute-start.13
  545.3 6.1 collective-permute-start.14
  546.6 5.3 collective-permute-start.15
  551.3 1.5 copy-start.35
  551.4 1.5 copy-start.36
  598.6 11.2 %slice-start = ((f32[4,4,4]{2,0,1:T(4,128)}), f32[4,3,4]{2,0,1:T(4,128)S(1)}, s32[]{:S(2)}) async-start(f32[4,4,4]{2,0,1:T(4,128)} %copy-done.51), calls=%async_computation.3 | async-start | bytes 12288 | tf_op jit(solution)/shard_map/slice | solution.py:136
  598.6 11.2 %copy-start.66 = (f32[4,1,4]{2,0,1:T(4,128)S(1)}, f32[4,1,4]{2,0,1:T(4,128)}, u32[]{:S(2)}) copy-start(f32[4,1,4]{2,0,1:T(4,128)} %slice.1403) | copy-start | bytes 196
  598.6 20.7 %all-to-all-start.2 = ((f32[64,4,4]{2,1,0:T(4,128)}), f32[64,4,4]{2,1,0:T(4,128)S(1)}, u32[]{:S(2)}, u32[]{:S(2)}) async-start(f32[64,4,4]{2,1,0:T(4,128)} %copy.273), calls=%async_computation.2 | async-start | bytes 262144 | tf_op jit(solution)/shard_map/all_to_all | solution.py:126
  610.0 9.3 %copy-start.65 = (s32[64]{0:T(128)S(1)}, s32[64]{0:T(128)}, u32[]{:S(2)}) copy-start(s32[64]{0:T(128)} %eq.29) | copy-start | bytes 772
  (49 other events, 43.6 us)
